TPU v7x, 256 devices: a whole 4x4x8 slice. The times are simulated.
256 devices in a mesh: section: 4 (over x), adapter: 2 (over core), mp: 32 (over z, y).
Axes of the slice: x: 4, y: 4, z: 8, core: 2. Of those that a mesh axis runs over, the one named last changes fastest.
Arguments:
- forward_input: bfloat16 [4, 2048, 8192], P('section', 'adapter', 'mp'), may hold values from -6 to 6
- stored_input: bfloat16 [4, 2048, 8192], P('section', 'adapter', 'mp'), may hold values from -6 to 6
- output_gradient: bfloat16 [4, 2048, 8192], P('section', 'adapter', 'mp'), may hold values from -6 to 6
- frozen_weight: bfloat16 [4, 8192, 8192], P('section', None, 'mp'), may hold values from -0.0625 to 0.0625
- adapter_down_factor: bfloat16 [4, 16, 64, 8192], P('section', 'adapter', None, 'mp'), may hold values from -0.0625 to 0.0625
- adapter_up_factor: bfloat16 [4, 16, 64, 8192], P('section', 'adapter', None, 'mp'), may hold values from -0.0625 to 0.0625
- adapter_index_list: int32 [2, 4, 16], P(None, 'section', 'adapter'), may hold values from 0 to 15, as said below
Outputs:
- fwd_out: bfloat16 [4, 2048, 8192], P('section', 'adapter', 'mp')
- grad_in: bfloat16 [4, 2048, 8192], P('section', 'adapter', 'mp')
- grad_a: bfloat16 [4, 16, 64, 8192], P('section', 'adapter', None, 'mp')
- grad_b: bfloat16 [4, 16, 64, 8192], P('section', 'adapter', None, 'mp')
Inputs may be any that keep to these rules, and one draw needn't show every extreme that they name: `adapter_index_list`: owner o holds adapters o * 8 to (o + 1) * 8 - 1. Of the 8 sequences of one index of the adapter axis, for one segment and one micro-batch, at most 5 use adapters of one owner; for each segment and micro-batch one owner gets exactly 5 from every index.
All inputs are finite; a program needn't handle non-finite values.
Results may differ from a plain program's by a relative error of at most 0.013.
Values may be sent and summed in bfloat16 or wider, within the bound.
No kernel may reach another device: no remote copies, remote signals or barrier semaphores. Data moves between devices by JAX's collectives and lax.ppermute only.
A program may use at most 128 MiB of HBM per device.

v0:
```python
import jax
import jax.numpy as jnp
from jax import lax
from jax.sharding import PartitionSpec as P

adapter_scale = 2.0


def shifted(value, axis, steps):
    count = lax.axis_size(axis)
    pairs = [(source, (source + steps) % count) for source in range(count)]
    return lax.ppermute(value, axis, pairs)


def pack_slots(ids_row, capacity, owners_count, adapters_held):
    seq_count = ids_row.shape[0]
    owners = ids_row // adapters_held
    positions = jnp.arange(seq_count, dtype=jnp.int32)
    same_owner = owners[:, None] == owners[None, :]
    earlier = positions[None, :] < positions[:, None]
    slot_rank = jnp.sum((same_owner & earlier).astype(jnp.int32), axis=1)
    slot_index = owners * capacity + slot_rank
    slot_ids = jnp.arange(owners_count * capacity, dtype=jnp.int32)
    placing = (slot_index[None, :] == slot_ids[:, None]).astype(jnp.bfloat16)
    local_ids = ids_row % adapters_held
    pick_seq = (local_ids[:, None] == jnp.arange(adapters_held, dtype=jnp.int32)[None, :]).astype(
        jnp.bfloat16
    )
    chosen = jnp.dot(placing, pick_seq, preferred_element_type=jnp.float32).astype(jnp.bfloat16)
    return (placing, chosen.reshape(owners_count, capacity, adapters_held))


def select_slabs(chosen, table):
    return jnp.einsum("nkj,jrm->nkrm", chosen, table, preferred_element_type=jnp.float32).astype(
        jnp.bfloat16
    )


def local(
    forward_input,
    stored_input,
    output_gradient,
    frozen_weight,
    adapter_down_factor,
    adapter_up_factor,
    adapter_index_list,
):
    single_float = jnp.float32
    brain_half_float = jnp.bfloat16
    highest_accuracy = lax.Precision.HIGHEST
    owners_count = lax.axis_size("adapter")
    seq_count = adapter_index_list.shape[2]
    capacity = max(2, seq_count // owners_count + 1)
    slot_total = owners_count * capacity
    hidden_state = forward_input[0]
    saved = stored_input[0]
    cotangent = output_gradient[0]
    weight = frozen_weight[0]
    down_factor_table = adapter_down_factor[0]
    up_factor_table = adapter_up_factor[0]
    adapters_held = down_factor_table.shape[0]
    rows, width = hidden_state.shape
    seq_len = rows // seq_count
    forward_base_output = jnp.dot(
        lax.all_gather(hidden_state, "mp", axis=1, tiled=True),
        weight,
        preferred_element_type=single_float,
    )
    back_term = lax.dot_general(
        cotangent, weight, (((1,), (1,)), ((), ())), preferred_element_type=single_float
    )
    base_back = lax.psum_scatter(
        back_term.astype(jnp.bfloat16), "mp", scatter_dimension=1, tiled=True
    ).astype(jnp.float32)
    forward_placement, pick_fwd = pack_slots(
        adapter_index_list[0, 0], capacity, owners_count, adapters_held
    )
    placing_back, pick_back = pack_slots(
        adapter_index_list[1, 0], capacity, owners_count, adapters_held
    )

    def to_slots(placing, values):
        flat_rows = values.reshape(seq_count, seq_len * width)
        packed = jnp.dot(placing, flat_rows, preferred_element_type=single_float).astype(
            brain_half_float
        )
        return packed.reshape(owners_count, capacity, seq_len, width)

    def slots_gathered(placing, values):
        flat_rows = values.reshape(slot_total, seq_len * width)
        spread = lax.dot_general(
            placing, flat_rows, (((0,), (0,)), ((), ())), preferred_element_type=single_float
        )
        return spread.reshape(rows, width)

    send_fwd = to_slots(forward_placement, hidden_state)
    send_saved = to_slots(placing_back, saved)
    send_grad = to_slots(placing_back, cotangent)
    rows_fwd = lax.all_to_all(send_fwd, "adapter", split_axis=0, concat_axis=0, tiled=True)
    rows_saved = lax.all_to_all(send_saved, "adapter", split_axis=0, concat_axis=0, tiled=True)
    token_row_gradient = lax.all_to_all(
        send_grad, "adapter", split_axis=0, concat_axis=0, tiled=True
    )
    owner_fwd = lax.all_to_all(pick_fwd, "adapter", split_axis=0, concat_axis=0, tiled=True)
    owner_back = lax.all_to_all(pick_back, "adapter", split_axis=0, concat_axis=0, tiled=True)
    first_fwd = select_slabs(owner_fwd, down_factor_table)
    second_fwd = select_slabs(owner_fwd, up_factor_table)
    first_back = select_slabs(owner_back, down_factor_table)
    second_back = select_slabs(owner_back, up_factor_table)
    rank_fwd = jnp.einsum(
        "nklm,nkrm->nkrl", rows_fwd, first_fwd, preferred_element_type=single_float
    )
    rank_back = jnp.einsum(
        "nklm,nkrm->nkrl", rows_saved, first_back, preferred_element_type=single_float
    )
    rank_space_gradient = jnp.einsum(
        "nklm,nkrm->nkrl", token_row_gradient, second_back, preferred_element_type=single_float
    )
    rank_fwd, rank_back, rank_space_gradient = lax.psum(
        (rank_fwd, rank_back, rank_space_gradient), "mp"
    )
    coded_fwd = rank_fwd.astype(brain_half_float)
    encoded_backward = rank_back.astype(brain_half_float)
    gradient_scaled = (adapter_scale * rank_space_gradient).astype(brain_half_float)
    adapter_token_rows = jnp.einsum(
        "nkrl,nkrm->nklm", coded_fwd, second_fwd, preferred_element_type=single_float
    ).astype(brain_half_float)
    back_rows = jnp.einsum(
        "nkrl,nkrm->nklm", gradient_scaled, first_back, preferred_element_type=single_float
    ).astype(brain_half_float)
    adapter_home_output = lax.all_to_all(
        adapter_token_rows, "adapter", split_axis=0, concat_axis=0, tiled=True
    )
    returned_home = lax.all_to_all(back_rows, "adapter", split_axis=0, concat_axis=0, tiled=True)
    slot_down_gradient = jnp.einsum(
        "nkrl,nklm->nkrm", gradient_scaled, rows_saved, preferred_element_type=single_float
    )
    slot_up_gradient = adapter_scale * jnp.einsum(
        "nkrl,nklm->nkrm", encoded_backward, token_row_gradient, preferred_element_type=single_float
    )
    adapter_home_output, returned_home, slot_down_gradient, slot_up_gradient, owner_selection = (
        adapter_home_output,
        returned_home,
        slot_down_gradient,
        slot_up_gradient,
        owner_back,
    )
    owner_weights = owner_selection.astype(single_float)
    grad_a = (
        jnp.einsum("nkj,nkrm->jrm", owner_weights, slot_down_gradient, precision=highest_accuracy)
        / seq_len
    ).astype(brain_half_float)
    grad_b = (
        jnp.einsum("nkj,nkrm->jrm", owner_weights, slot_up_gradient, precision=highest_accuracy)
        / seq_len
    ).astype(brain_half_float)
    adapter_sequence_output = slots_gathered(forward_placement, adapter_home_output)
    back_seq = slots_gathered(placing_back, returned_home)
    forward_output = (
        hidden_state.astype(single_float)
        + forward_base_output
        + adapter_scale * adapter_sequence_output
    ).astype(brain_half_float)
    out_back = (cotangent.astype(single_float) + base_back + back_seq).astype(brain_half_float)
    fwd_next = shifted(forward_output, "section", 1)
    back_next = shifted(out_back, "section", -1)
    return (fwd_next[None], back_next[None], grad_a[None], grad_b[None])


def solution(mesh):
    in_specs = (
        P("section", "adapter", "mp"),
        P("section", "adapter", "mp"),
        P("section", "adapter", "mp"),
        P("section", None, "mp"),
        P("section", "adapter", None, "mp"),
        P("section", "adapter", None, "mp"),
        P(None, "section", "adapter"),
    )
    out_specs = (
        P("section", "adapter", "mp"),
        P("section", "adapter", "mp"),
        P("section", "adapter", None, "mp"),
        P("section", "adapter", None, "mp"),
    )
    return jax.shard_map(local, mesh=mesh, in_specs=in_specs, out_specs=out_specs, check_vma=False)
```

profile of v0, /device:TPU:1, one launch (start us, length us, event | category | flops | bytes accessed | tf_op | source)
XLA Modules:
  0.0 587.1 jit_solution(10407722056078918129)
XLA Ops:
  7.2 0.7 and_select_fusion
  7.9 0.7 and_select_fusion.1
  8.6 0.2 convert_reduce_fusion
  8.8 0.3 convolution_convert_fusion.9
  9.1 0.1 reshape.218
  9.1 0.7 copy.70
  9.8 6.4 %all-to-all-start.3 = ((bf16[2,5,8]{2,1,0:T(8,128)(2,1)}), bf16[2,5,8]{2,1,0:T(8,128)(2,1)S(1)}, u32[]{:S(2)}, u32[]{:S(2)}) async-start(bf16[2,5,8]{2,1,0:T(8,128)(2,1)} %copy.70), calls=%async_computation.4 | async-start | bytes 8192 | tf_op jit(solution)/shard_map/all_to_all | solution.py:105
  16.2 1.3 reshape_squeeze.10
  17.5 0.4 convolution_convert_fusion.1
  18.0 0.2 copy.96
  18.2 0.9 slice.9
  19.1 3.5 all-to-all-start.4
  22.7 0.3 convolution_convert_fusion.6
  23.0 1.1 all-to-all-done.4
  24.1 1.1 fusion.28
  25.2 0.7 all-gather.3.cloned.1.call-update
  26.0 10.3 %convolution_convert_fusion.3 = bf16[1024,8192]{1,0:T(8,128)(2,1)} fusion(bf16[1,8192,256]{2,1,0:T(8,128)(2,1)} %param.10, bf16[1,1024,256]{2,1,0:T(8,128)(2,1)S(1)} %copy-done), kind=kOutput, calls=%fused_computation.6 | convolution fusion | flops 4303355904 | bytes 21495808 | tf_op jit(solution)/shard_map/dot_general | solution.py:69
  36.4 1.0 copy-done.6
  37.4 0.2 reshape_squeeze.11
  37.6 0.4 convolution_convert_fusion
  38.1 0.2 copy.98
  38.3 0.9 slice.10
  39.2 3.9 all-to-all-start.6
  43.0 0.2 reshape_squeeze.9
  43.3 0.3 convolution_convert_fusion.10
  43.5 0.1 reshape.215
  43.6 0.6 copy.63
  44.2 1.2 fusion.35
  45.5 3.2 all-to-all-start
  48.7 1.1 fusion.65
  49.8 0.4 convolution_convert_fusion.2
  50.2 0.2 copy.94
  50.5 0.9 slice.8
  51.3 3.5 all-to-all-start.1
  54.9 2.1 convolution_convert_fusion.8
  57.0 2.1 fusion.31
  59.1 123.4 %all-reduce.5 = (bf16[2,5,64,128]{3,2,1,0:T(8,128)(2,1)}, bf16[2,5,64,128]{3,2,1,0:T(8,128)(2,1)}) all-reduce(f32[2,5,64,128]{3,2,1,0:T(8,128)} %fusion.31, f32[2,5,64,128]{3,2,1,0:T(8,128)S(1)} %copy-done.3), channel_id=1, replica_groups=mesh['section'=4,'adapter'=2,'mp'=32] {'mp'}, use_global_device_ids=true, to_apply=%region_1.2 | all-reduce | flops 163840 | bytes 983040 | tf_op jit(solution)/shard_map/psum | solution.py:119
  182.5 1.3 convolution_convert_fusion.7
  183.8 1.3 convolution_convert_fusion.5
  185.1 32.4 %all_to_all.35 = bf16[2,5,128,256]{3,2,1,0:T(8,128)(2,1)S(1)} all-to-all(bf16[2,5,128,256]{3,2,1,0:T(8,128)(2,1)S(1)} %convolution_convert_fusion.5), channel_id=1, replica_groups=mesh['section'=4,'adapter'=2,'mp'=32] {'adapter'}, dimensions={0} | all-to-all | bytes 1310720 | tf_op jit(solution)/shard_map/all_to_all | solution.py:131
  217.6 0.6 copy.95
  218.2 0.4 convolution_multiply_fusion
  218.5 1.1 mul.38
  219.7 1.1 convolution_multiply_fusion.1
  220.8 1.4 convolution_convert_fusion.4
  222.2 4.3 all_to_all.36
  226.5 0.1 pad.1
  226.6 0.6 copy.97
  227.2 0.4 fusion.45
  227.6 1.1 reshape.221
  228.7 91.3 %all-gather.3.cloned.1.call-done = bf16[1,1024,8192]{2,1,0:T(8,128)(2,1)} async-done(((bf16[1,1024,256]{2,1,0:T(8,128)(2,1)}), bf16[1,1024,8192]{2,1,0:T(8,128)(2,1)}) %all-gather.3.cloned.1.call-update) | async-done | bytes 16777232 | tf_op jit(solution)/shard_map/all_gather | solution.py:65
  320.0 12.7 %fusion.14 = bf16[1024,256]{1,0:T(8,128)(2,1)} fusion(f32[1024,256]{1,0:T(8,128)} %mul.38, bf16[1,8192,256]{2,1,0:T(8,128)(2,1)} %param.10, bf16[1,1024,8192]{2,1,0:T(8,128)(2,1)} %all-gather.3.cloned.1.call-done, bf16[1,1024,256]{2,1,0:T(8,128)(2,1)} %param.7), kind=kOutput, calls=%fused_computation.13 | convolution fusion | flops 4296015872 | bytes 23068672 | tf_op jit(solution)/shard_map/dot_general | solution.py:64
  332.6 1.2 collective-permute-start
  333.8 234.2 %reduce-scatter.2.cloned.1.call-done = bf16[1024,256]{1,0:T(8,128)(2,1)} async-done(((bf16[1024,8192]{1,0:T(8,128)(2,1)}), bf16[1024,256]{1,0:T(8,128)(2,1)}) %reduce-scatter.2.cloned.1.call-update) | async-done | bytes 524304 | tf_op jit(solution)/shard_map/reduce_scatter | solution.py:72
  568.0 1.2 add_convert_fusion
  569.2 2.5 collective-permute-start.1
  571.8 1.1 fusion.23
  572.9 0.8 copy.80
  573.6 0.2 fusion.44
  573.9 1.1 fusion.24
  575.0 0.8 copy.79
  575.7 2.2 collective-permute-done.1
  577.9 1.9 copy.138
  579.8 0.8 copy.139
  (27 shorter events, 0.3 us)
Async XLA Ops:
  7.2 15.5 %copy-start.5 = (bf16[1,8,64,256]{3,2,1,0:T(8,128)(2,1)S(1)}, bf16[1,8,64,256]{3,2,1,0:T(8,128)(2,1)}, u32[]{:S(2)}) copy-start(bf16[1,8,64,256]{3,2,1,0:T(8,128)(2,1)} %param.12) | copy-start | bytes 786436
  9.8 9.3 %all-to-all-start.3 = ((bf16[2,5,8]{2,1,0:T(8,128)(2,1)}), bf16[2,5,8]{2,1,0:T(8,128)(2,1)S(1)}, u32[]{:S(2)}, u32[]{:S(2)}) async-start(bf16[2,5,8]{2,1,0:T(8,128)(2,1)} %copy.70), calls=%async_computation.4 | async-start | bytes 8192 | tf_op jit(solution)/shard_map/all_to_all | solution.py:105
  18.0 8.0 %copy-start = (bf16[1,1024,256]{2,1,0:T(8,128)(2,1)S(1)}, bf16[1,1024,256]{2,1,0:T(8,128)(2,1)}, u32[]{:S(2)}) copy-start(bf16[1,1024,256]{2,1,0:T(8,128)(2,1)} %param.9) | copy-start | bytes 1572868
  19.1 5.0 all-to-all-start.4
  22.6 198.2 %all-reduce.4.cloned.1.call-start = ((), (), s32[]{:S(2)}) async-start(), calls=%async_computation.9 | async-start | bytes 655360 | tf_op jit(solution)/shard_map/psum | solution.py:119
  25.2 294.8 %all-gather.3.cloned.1.call-start = ((), (), s32[]{:S(2)}) async-start(), calls=%async_computation.10 | async-start | bytes 17301504 | tf_op jit(solution)/shard_map/all_gather | solution.py:65
  25.9 542.1 %reduce-scatter.2.cloned.1.call-start = ((), (), s32[]{:S(2)}) async-start(), calls=%async_computation.8 | async-start | bytes 17301504 | tf_op jit(solution)/shard_map/reduce_scatter | solution.py:72
  36.3 1.0 copy-start.6
  37.4 5.6 copy-start.2
  39.2 6.3 %all-to-all-start.6 = ((bf16[2,5,128,256]{3,2,1,0:T(8,128)(2,1)}), bf16[2,5,128,256]{3,2,1,0:T(8,128)(2,1)S(1)}, u32[]{:S(2)}, u32[]{:S(2)}) async-start(bf16[2,5,128,256]{3,2,1,0:T(8,128)(2,1)} %bitcast.51), calls=%async_computation.7 | async-start | bytes 1310720 | tf_op jit(solution)/shard_map/all_to_all | solution.py:100
  45.5 5.9 all-to-all-start
  50.2 8.9 %copy-start.3 = (f32[2,5,64,128]{3,2,1,0:T(8,128)S(1)}, f32[2,5,64,128]{3,2,1,0:T(8,128)}, u32[]{:S(2)}) copy-start(f32[2,5,64,128]{3,2,1,0:T(8,128)} %fusion.65) | copy-start | bytes 983044
  51.3 5.6 all-to-all-start.1
  228.7 339.3 %copy-start.1 = (f32[1024,256]{1,0:T(8,128)S(1)}, f32[1024,256]{1,0:T(8,128)}, u32[]{:S(2)}) copy-start(f32[1024,256]{1,0:T(8,128)} %reshape.221) | copy-start | bytes 3145732
  332.6 241.0 %copy-start.4 = (f32[2,5,64,128]{3,2,1,0:T(8,128)S(1)}, f32[2,5,64,128]{3,2,1,0:T(8,128)}, u32[]{:S(2)}) copy-start(f32[2,5,64,128]{3,2,1,0:T(8,128)} %all-reduce.4.cloned.1.call-done) | copy-start | bytes 983044
  332.6 243.1 %collective-permute-start = (bf16[1024,256]{1,0:T(8,128)(2,1)}, bf16[1024,256]{1,0:T(8,128)(2,1)}, u32[]{:S(2)}, u32[]{:S(2)}) collective-permute-start(bf16[1024,256]{1,0:T(8,128)(2,1)} %fusion.14), channel_id=1, source_target_pairs={{0,64},{64,128},{128,192},{192,0},{1,65},{65,129},{129,193},{193,1... | collective-permute-start | bytes 1572872 | tf_op jit(solution)/shard_map/ppermute | solution.py:12
  569.2 8.6 %collective-permute-start.1 = (bf16[1024,256]{1,0:T(8,128)(2,1)S(1)}, bf16[1024,256]{1,0:T(8,128)(2,1)S(1)}, u32[]{:S(2)}, u32[]{:S(2)}) collective-permute-start(bf16[1024,256]{1,0:T(8,128)(2,1)S(1)} %add_convert_fusion), channel_id=1, source_target_pairs={{0,192},{64,0},{128,64},{192,128},{1,193},{65,1},{129,65},{193,129... | collective-permute-start | bytes 1572872 | tf_op jit(solution)/shard_map/ppermute | solution.py:12
Sparse Core Ops, SparseCore 0:
  26.9 142.4 all-reduce.3
  171.9 148.0 all-gather.2
  324.1 243.9 reduce-scatter.1
where the time goes:
time: 594 us; the launch traced here: 587 us
  waiting for transfers between devices  330 us (56%)
  blocking collectives  160 us (27%)
  matrix products  40.9 us (7%)
  starting transfers between devices  24.4 us (4%)
  local copies, waits for them, and re-layouts  15.3 us (3%)
  between operations  14 us (2%)
    reduce_scatter x1, waiting for transfers between devices, local(): lax.psum_scatter(back_term.astype(jnp.bfloat16), 'mp', scatter_dimension=...  234 us
    psum x1, blocking collectives, local(): lax.psum((rank_fwd, rank_back, rank_space_gradient), 'mp')  123 us
    all_gather x1, waiting for transfers between devices, local(): lax.all_gather(hidden_state, 'mp', axis=1, tiled=True)  91.3 us
    all_to_all x1, blocking collectives, local(): lax.all_to_all(adapter_token_rows, 'adapter', split_axis=0, concat_axis=0...  32.4 us
    dot_general x1, matrix products, local(): jnp.dot(lax.all_gather(hidden_state, 'mp', axis=1, tiled=True), weight, p...  12.7 us
  transfers between devices with their start and end apart: 10, of which 4 were waited for; matrix products, arithmetic and copies ran while one was open for 9% of the time, Pallas kernels for 0%

commit v1 on v0

--- a/solution.py
+++ b/solution.py
@@ -10,6 +10,42 @@
     count = lax.axis_size(axis)
     pairs = [(source, (source + steps) % count) for source in range(count)]
     return lax.ppermute(value, axis, pairs)
+
+
+def exchange(value, axis, bit):
+    count = lax.axis_size(axis)
+    pairs = [(source, source ^ (1 << bit)) for source in range(count)]
+    return lax.ppermute(value, axis, pairs)
+
+
+def halving_doubling_sum(values, axis):
+    count = lax.axis_size(axis)
+    levels = count.bit_length() - 1
+    assert 1 << levels == count
+    order = [0, 2, 1, 3, 4, 5, 6, 7, 8][:levels] if levels >= 3 else list(range(levels))
+    order = [b for b in order if b < levels]
+    me = lax.axis_index(axis)
+    flat = jnp.concatenate([v.reshape(-1) for v in values])
+    total = flat.shape[0]
+    assert total % count == 0
+    held = flat
+    for bit in order:
+        half = held.shape[0] // 2
+        low, high = held[:half], held[half:]
+        upper = ((me >> bit) & 1) == 1
+        keep = jnp.where(upper, high, low)
+        send = jnp.where(upper, low, high)
+        held = keep + exchange(send, axis, bit)
+    for bit in reversed(order):
+        upper = ((me >> bit) & 1) == 1
+        other = exchange(held, axis, bit)
+        held = jnp.where(upper, jnp.concatenate([other, held]), jnp.concatenate([held, other]))
+    pieces = []
+    start = 0
+    for v in values:
+        pieces.append(held[start:start + v.size].reshape(v.shape))
+        start += v.size
+    return tuple(pieces)
 
 
 def pack_slots(ids_row, capacity, owners_count, adapters_held):
@@ -116,7 +152,7 @@
     rank_space_gradient = jnp.einsum(
         "nklm,nkrm->nkrl", token_row_gradient, second_back, preferred_element_type=single_float
     )
-    rank_fwd, rank_back, rank_space_gradient = lax.psum(
+    rank_fwd, rank_back, rank_space_gradient = halving_doubling_sum(
         (rank_fwd, rank_back, rank_space_gradient), "mp"
     )
     coded_fwd = rank_fwd.astype(brain_half_float)

time: 594 us -> 448 us (0.75)
  blocking collectives: 160 us -> 17.4 us
  waiting for transfers between devices: 330 us -> 303 us
  starting transfers between devices: 24.4 us -> 49.4 us
    psum x1 -> x0, blocking collectives: 123 us -> none  [local(): lax.psum((rank_fwd, rank_back, rank_space_gradient), 'mp')]
    all_gather x1, waiting for transfers between devices: 91.3 us -> 0.02 us  [local(): lax.all_gather(hidden_state, 'mp', axis=1, tiled=True)]
    ppermute x0 -> x10, waiting for transfers between devices: none -> 69.4 us  [exchange(): return lax.ppermute(value, axis, pairs)]
    all_to_all x1, blocking collectives: 32.4 us -> 4.28 us  [local(): lax.all_to_all(adapter_token_rows, 'adapter', split_axis=0, concat_axis=0...]
    ppermute x0 -> x10, starting transfers between devices: none -> 23.5 us  [exchange(): return lax.ppermute(value, axis, pairs)]
    all_to_all x1, blocking collectives: 4.32 us -> 13.1 us  [local(): lax.all_to_all(back_rows, 'adapter', split_axis=0, concat_axis=0, tiled=T...]
  transfers between devices with their start and end apart: 10 -> 19, of which waited for: 4 -> 15; matrix products, arithmetic and copies ran while one was open for 9% -> 12% of each run, Pallas kernels for 0% -> 0%
where the time goes in v1:
time: 448 us; the launch traced here: 442 us
  waiting for transfers between devices  303 us (68%)
  starting transfers between devices  49.4 us (11%)
  matrix products  38.3 us (9%)
  blocking collectives  17.4 us (4%)
  local copies, waits for them, and re-layouts  16.4 us (4%)
  between operations  14.4 us (3%)
    reduce_scatter x1, waiting for transfers between devices, local(): lax.psum_scatter(back_term.astype(jnp.bfloat16), 'mp', scatter_dimension=...  229 us
    ppermute x10, waiting for transfers between devices, exchange(): return lax.ppermute(value, axis, pairs)  69.4 us
    ppermute x10, starting transfers between devices, exchange(): return lax.ppermute(value, axis, pairs)  23.5 us
    all_to_all x1, blocking collectives, local(): lax.all_to_all(back_rows, 'adapter', split_axis=0, concat_axis=0, tiled=T...  13.1 us
    dot_general x1, matrix products, local(): jnp.dot(lax.all_gather(hidden_state, 'mp', axis=1, tiled=True), weight, p...  12.7 us
    dot_general x1, matrix products, local(): lax.dot_general(cotangent, weight, (((1,), (1,)), ((), ())), preferred_el...  9.83 us
    unnamed x32, local copies, waits for them, and re-layouts  9.52 us
  transfers between devices with their start and end apart: 19, of which 15 were waited for; matrix products, arithmetic and copies ran while one was open for 12% of the time, Pallas kernels for 0%

profile of v1, /device:TPU:1, one launch (start us, length us, event | category | flops | bytes accessed | tf_op | source)
XLA Modules:
  0.0 442.3 jit_solution(13797555097661208737)
XLA Ops:
  7.2 0.7 all-gather.3.cloned.1.call-update
  7.9 9.8 %convolution_convert_fusion.3 = bf16[1024,8192]{1,0:T(8,128)(2,1)} fusion(bf16[1,8192,256]{2,1,0:T(8,128)(2,1)} %param.10, bf16[1,1024,256]{2,1,0:T(8,128)(2,1)} %param.9), kind=kOutput, calls=%fused_computation.6 | convolution fusion | flops 4303355904 | bytes 21495808 | tf_op jit(solution)/shard_map/dot_general | solution.py:105
  17.8 0.6 copy-done.8
  19.0 0.7 copy.65
  19.7 6.4 %all-to-all-start = ((bf16[2,5,8]{2,1,0:T(8,128)(2,1)}), bf16[2,5,8]{2,1,0:T(8,128)(2,1)S(1)}, u32[]{:S(2)}, u32[]{:S(2)}) async-start(bf16[2,5,8]{2,1,0:T(8,128)(2,1)} %copy.65), calls=%async_computation | async-start | bytes 8192 | tf_op jit(solution)/shard_map/all_to_all | solution.py:141
  26.9 0.4 convolution_convert_fusion.2
  27.6 0.9 slice.76
  28.5 0.4 convolution_convert_fusion.1
  29.1 0.9 slice.77
  30.4 0.6 copy.70
  31.0 0.4 convolution_convert_fusion
  31.6 0.9 slice.78
  32.5 3.2 all-to-all-start.3
  36.1 1.1 convolution_convert_fusion.8
  37.2 3.5 all-to-all-start.1
  40.7 1.1 convolution_convert_fusion.7
  41.9 0.3 all-to-all-done.1
  42.2 3.9 all-to-all-start.2
  46.1 0.4 fusion.70
  46.4 1.1 all-to-all-done.2
  47.5 4.6 %all-to-all-start.4 = ((bf16[2,5,128,256]{3,2,1,0:T(8,128)(2,1)}), bf16[2,5,128,256]{3,2,1,0:T(8,128)(2,1)}, u32[]{:S(2)}, u32[]{:S(2)}) async-start(bf16[2,5,128,256]{3,2,1,0:T(8,128)(2,1)} %bitcast.167), calls=%async_computation.4 | async-start | bytes 1310720 | tf_op jit(solution)/shard_map/all_to_all | solution.py:135
  52.2 1.4 fusion.32
  53.8 1.6 fusion.30
  55.5 12.5 %collective-permute-done = f32[122880]{0:T(1024)} collective-permute-done((f32[122880]{0:T(1024)S(1)}, f32[122880]{0:T(1024)}, u32[]{:S(2)}, u32[]{:S(2)}) %collective-permute-start) | collective-permute-done | bytes 491552 | tf_op jit(solution)/shard_map/ppermute | solution.py:18
  68.0 1.1 select_add_fusion
  69.3 6.3 %collective-permute-done.1 = f32[61440]{0:T(1024)S(1)} collective-permute-done((f32[61440]{0:T(1024)S(1)}, f32[61440]{0:T(1024)S(1)}, u32[]{:S(2)}, u32[]{:S(2)}) %collective-permute-start.1) | collective-permute-done | bytes 245792 | tf_op jit(solution)/shard_map/ppermute | solution.py:18
  75.6 1.6 collective-permute-start.2
  77.2 6.5 %collective-permute-done.2 = f32[30720]{0:T(1024)S(1)} collective-permute-done((f32[30720]{0:T(1024)S(1)}, f32[30720]{0:T(1024)S(1)}, u32[]{:S(2)}, u32[]{:S(2)}) %collective-permute-start.2) | collective-permute-done | bytes 122912 | tf_op jit(solution)/shard_map/ppermute | solution.py:18
  83.8 1.7 collective-permute-start.3
  85.5 3.3 collective-permute-done.3
  88.8 5.6 %collective-permute-start.4 = (f32[7680]{0:T(1024)S(1)}, f32[7680]{0:T(1024)S(1)}, u32[]{:S(2)}, u32[]{:S(2)}) collective-permute-start(f32[7680]{0:T(1024)S(1)} %slice_select_fusion.3), channel_id=1, source_target_pairs={{0,16},{1,17},{2,18},{3,19},{4,20},{5,21},{6,22},{7,23},{8,24},{9,... | collective-permute-start | bytes 92168 | tf_op jit(solution)/shard_map/ppermute | solution.py:18
  94.4 2.2 collective-permute-done.4
  96.6 5.5 %collective-permute-start.5 = (f32[7680]{0:T(1024)S(1)}, f32[7680]{0:T(1024)S(1)}, u32[]{:S(2)}, u32[]{:S(2)}) collective-permute-start(f32[7680]{0:T(1024)S(1)} %select_add_fusion.4), channel_id=1, source_target_pairs={{0,16},{1,17},{2,18},{3,19},{4,20},{5,21},{6,22},{7,23},{8,24},{9,... | collective-permute-start | bytes 92168 | tf_op jit(solution)/shard_map/ppermute | solution.py:18
  102.1 2.1 collective-permute-done.5
  104.3 3.8 collective-permute-start.6
  108.1 4.0 collective-permute-done.6
  112.1 3.7 collective-permute-start.7
  115.8 5.1 %collective-permute-done.7 = f32[30720]{0:T(1024)S(1)} collective-permute-done((f32[30720]{0:T(1024)S(1)}, f32[30720]{0:T(1024)S(1)}, u32[]{:S(2)}, u32[]{:S(2)}) %collective-permute-start.7) | collective-permute-done | bytes 122912 | tf_op jit(solution)/shard_map/ppermute | solution.py:18
  121.0 10.0 %collective-permute-done.8 = f32[61440]{0:T(1024)S(1)} collective-permute-done((f32[61440]{0:T(1024)S(1)}, f32[61440]{0:T(1024)S(1)}, u32[]{:S(2)}, u32[]{:S(2)}) %collective-permute-start.8) | collective-permute-done | bytes 245792 | tf_op jit(solution)/shard_map/ppermute | solution.py:18
  131.0 1.3 collective-permute-start.9
  132.4 2.1 convolution_convert_fusion.6
  134.5 17.4 %collective-permute-done.9 = f32[122880]{0:T(1024)S(1)} collective-permute-done((f32[122880]{0:T(1024)S(1)}, f32[122880]{0:T(1024)S(1)}, u32[]{:S(2)}, u32[]{:S(2)}) %collective-permute-start.9) | collective-permute-done | bytes 491552 | tf_op jit(solution)/shard_map/ppermute | solution.py:18
  152.0 0.4 convolution_convert_fusion.5
  152.4 13.1 %all_to_all.35 = bf16[2,5,128,256]{3,2,1,0:T(8,128)(2,1)S(1)} all-to-all(bf16[2,5,128,256]{3,2,1,0:T(8,128)(2,1)S(1)} %convolution_convert_fusion.5), channel_id=1, replica_groups=mesh['section'=4,'adapter'=2,'mp'=32] {'adapter'}, dimensions={0} | all-to-all | bytes 1310720 | tf_op jit(solution)/shard_map/all_to_all | solution.py:170
  165.6 0.6 copy.100
  166.2 1.3 fusion.49
  167.5 2.4 reshape.256
  169.9 0.4 convolution_convert_fusion.4
  170.3 4.3 all_to_all.36
  174.6 0.6 copy.99
  175.2 1.3 convolution_multiply_fusion
  176.6 2.4 mul.39
  179.2 12.7 %fusion.14 = bf16[1024,256]{1,0:T(8,128)(2,1)} fusion(f32[1024,256]{1,0:T(8,128)} %mul.39, bf16[1,8192,256]{2,1,0:T(8,128)(2,1)} %param.10, bf16[1,1024,8192]{2,1,0:T(8,128)(2,1)} %all-gather.3.cloned.1.call-done, bf16[1,1024,256]{2,1,0:T(8,128)(2,1)} %param.7), kind=kOutput, calls=%fused_computation.13 | convolution fusion | flops 4296015872 | bytes 23068672 | tf_op jit(solution)/shard_map/dot_general | solution.py:100
  191.8 1.3 collective-permute-start.10
  193.1 228.9 %reduce-scatter.2.cloned.1.call-done = bf16[1024,256]{1,0:T(8,128)(2,1)} async-done(((bf16[1024,8192]{1,0:T(8,128)(2,1)}), bf16[1024,256]{1,0:T(8,128)(2,1)}) %reduce-scatter.2.cloned.1.call-update) | async-done | bytes 524304 | tf_op jit(solution)/shard_map/reduce_scatter | solution.py:108
  422.0 1.5 add_convert_fusion
  423.6 2.8 collective-permute-start.11
  426.3 1.1 fusion.24
  427.5 0.8 copy.81
  428.4 1.1 fusion.23
  429.6 0.8 copy.82
  430.3 2.5 collective-permute-done.11
  432.8 1.9 copy.135
  434.6 0.8 copy.136
  (62 shorter events, 4.2 us)
Async XLA Ops:
  7.2 172.0 %all-gather.3.cloned.1.call-start = ((), (), s32[]{:S(2)}) async-start(), calls=%async_computation.9 | async-start | bytes 17301504 | tf_op jit(solution)/shard_map/all_gather | solution.py:101
  7.9 414.1 %reduce-scatter.2.cloned.1.call-start = ((), (), s32[]{:S(2)}) async-start(), calls=%async_computation.8 | async-start | bytes 17301504 | tf_op jit(solution)/shard_map/reduce_scatter | solution.py:108
  17.8 0.7 copy-start.8
  17.8 8.4 %copy-start = (bf16[1,1024,256]{2,1,0:T(8,128)(2,1)S(1)}, bf16[1,1024,256]{2,1,0:T(8,128)(2,1)}, u32[]{:S(2)}) copy-start(bf16[1,1024,256]{2,1,0:T(8,128)(2,1)} %param.9) | copy-start | bytes 1572868
  17.8 8.6 %copy-start.3 = (bf16[1,1024,256]{2,1,0:T(8,128)(2,1)S(1)}, bf16[1,1024,256]{2,1,0:T(8,128)(2,1)}, u32[]{:S(2)}) copy-start(bf16[1,1024,256]{2,1,0:T(8,128)(2,1)} %param.7) | copy-start | bytes 1572868
  17.8 8.9 %copy-start.7 = (bf16[1,1024,256]{2,1,0:T(8,128)(2,1)S(1)}, bf16[1,1024,256]{2,1,0:T(8,128)(2,1)}, u32[]{:S(2)}) copy-start(bf16[1,1024,256]{2,1,0:T(8,128)(2,1)} %param.8) | copy-start | bytes 1572868
  19.7 12.8 %all-to-all-start = ((bf16[2,5,8]{2,1,0:T(8,128)(2,1)}), bf16[2,5,8]{2,1,0:T(8,128)(2,1)S(1)}, u32[]{:S(2)}, u32[]{:S(2)}) async-start(bf16[2,5,8]{2,1,0:T(8,128)(2,1)} %copy.65), calls=%async_computation | async-start | bytes 8192 | tf_op jit(solution)/shard_map/all_to_all | solution.py:141
  28.9 6.9 %copy-start.5 = (bf16[1,8,64,256]{3,2,1,0:T(8,128)(2,1)S(1)}, bf16[1,8,64,256]{3,2,1,0:T(8,128)(2,1)}, u32[]{:S(2)}) copy-start(bf16[1,8,64,256]{3,2,1,0:T(8,128)(2,1)} %param.11) | copy-start | bytes 786436
  28.9 7.2 %copy-start.6 = (bf16[1,8,64,256]{3,2,1,0:T(8,128)(2,1)S(1)}, bf16[1,8,64,256]{3,2,1,0:T(8,128)(2,1)}, u32[]{:S(2)}) copy-start(bf16[1,8,64,256]{3,2,1,0:T(8,128)(2,1)} %param.12) | copy-start | bytes 786436
  32.5 4.7 %all-to-all-start.3 = ((bf16[2,5,8]{1,2,0:T(8,128)(2,1)}), bf16[2,5,8]{1,2,0:T(8,128)(2,1)S(1)}, u32[]{:S(2)}, u32[]{:S(2)}) async-start(bf16[2,5,8]{1,2,0:T(8,128)(2,1)} %copy.70), calls=%async_computation.3 | async-start | bytes 8192 | tf_op jit(solution)/shard_map/all_to_all | solution.py:140
  36.1 11.5 %copy-start.1 = (bf16[2,5,64,256]{3,1,2,0:T(8,128)(2,1)}, bf16[2,5,64,256]{3,1,2,0:T(8,128)(2,1)S(1)}, u32[]{:S(2)}) copy-start(bf16[2,5,64,256]{3,1,2,0:T(8,128)(2,1)S(1)} %fusion.38) | copy-start | bytes 983044
  37.2 5.0 %all-to-all-start.1 = ((bf16[2,5,128,256]{3,2,1,0:T(8,128)(2,1)}), bf16[2,5,128,256]{3,2,1,0:T(8,128)(2,1)S(1)}, u32[]{:S(2)}, u32[]{:S(2)}) async-start(bf16[2,5,128,256]{3,2,1,0:T(8,128)(2,1)} %bitcast.39), calls=%async_computation.1 | async-start | bytes 1310720 | tf_op jit(solution)/shard_map/all_to_all | solution.py:136
  42.2 5.3 %all-to-all-start.2 = ((bf16[2,5,128,256]{3,2,1,0:T(8,128)(2,1)}), bf16[2,5,128,256]{3,2,1,0:T(8,128)(2,1)S(1)}, u32[]{:S(2)}, u32[]{:S(2)}) async-start(bf16[2,5,128,256]{3,2,1,0:T(8,128)(2,1)} %bitcast.43), calls=%async_computation.2 | async-start | bytes 1310720 | tf_op jit(solution)/shard_map/all_to_all | solution.py:137
  47.5 6.2 %all-to-all-start.4 = ((bf16[2,5,128,256]{3,2,1,0:T(8,128)(2,1)}), bf16[2,5,128,256]{3,2,1,0:T(8,128)(2,1)}, u32[]{:S(2)}, u32[]{:S(2)}) async-start(bf16[2,5,128,256]{3,2,1,0:T(8,128)(2,1)} %bitcast.167), calls=%async_computation.4 | async-start | bytes 1310720 | tf_op jit(solution)/shard_map/all_to_all | solution.py:135
  55.4 12.6 %collective-permute-start = (f32[122880]{0:T(1024)S(1)}, f32[122880]{0:T(1024)}, u32[]{:S(2)}, u32[]{:S(2)}) collective-permute-start(f32[122880]{0:T(1024)S(1)} %fusion.34), channel_id=1, source_target_pairs={{0,1},{1,0},{2,3},{3,2},{4,5},{5,4},{6,7},{7,6},{8,9},{9,8},{10,11... | collective-permute-start | bytes 1474568 | tf_op jit(solution)/shard_map/ppermute | solution.py:18
  69.1 82.9 %copy-start.2 = (bf16[2,5,64,256]{3,1,2,0:T(8,128)(2,1)S(1)}, bf16[2,5,64,256]{3,1,2,0:T(8,128)(2,1)}, u32[]{:S(2)}) copy-start(bf16[2,5,64,256]{3,1,2,0:T(8,128)(2,1)} %copy-done.1) | copy-start | bytes 983044
  69.2 6.4 %collective-permute-start.1 = (f32[61440]{0:T(1024)S(1)}, f32[61440]{0:T(1024)S(1)}, u32[]{:S(2)}, u32[]{:S(2)}) collective-permute-start(f32[61440]{0:T(1024)S(1)} %slice_select_fusion), channel_id=1, source_target_pairs={{0,4},{1,5},{2,6},{3,7},{4,0},{5,1},{6,2},{7,3},{8,12},{9,13},{10,... | collective-permute-start | bytes 737288 | tf_op jit(solution)/shard_map/ppermute | solution.py:18
  75.6 8.1 %collective-permute-start.2 = (f32[30720]{0:T(1024)S(1)}, f32[30720]{0:T(1024)S(1)}, u32[]{:S(2)}, u32[]{:S(2)}) collective-permute-start(f32[30720]{0:T(1024)S(1)} %slice_select_fusion.1), channel_id=1, source_target_pairs={{0,2},{1,3},{2,0},{3,1},{4,6},{5,7},{6,4},{7,5},{8,10},{9,11},{10,... | collective-permute-start | bytes 368648 | tf_op jit(solution)/shard_map/ppermute | solution.py:18
  83.8 5.0 %collective-permute-start.3 = (f32[15360]{0:T(1024)S(1)}, f32[15360]{0:T(1024)S(1)}, u32[]{:S(2)}, u32[]{:S(2)}) collective-permute-start(f32[15360]{0:T(1024)S(1)} %slice_select_fusion.2), channel_id=1, source_target_pairs={{0,8},{1,9},{2,10},{3,11},{4,12},{5,13},{6,14},{7,15},{8,0},{9,1},... | collective-permute-start | bytes 184328 | tf_op jit(solution)/shard_map/ppermute | solution.py:18
  88.8 7.8 %collective-permute-start.4 = (f32[7680]{0:T(1024)S(1)}, f32[7680]{0:T(1024)S(1)}, u32[]{:S(2)}, u32[]{:S(2)}) collective-permute-start(f32[7680]{0:T(1024)S(1)} %slice_select_fusion.3), channel_id=1, source_target_pairs={{0,16},{1,17},{2,18},{3,19},{4,20},{5,21},{6,22},{7,23},{8,24},{9,... | collective-permute-start | bytes 92168 | tf_op jit(solution)/shard_map/ppermute | solution.py:18
  96.6 7.7 %collective-permute-start.5 = (f32[7680]{0:T(1024)S(1)}, f32[7680]{0:T(1024)S(1)}, u32[]{:S(2)}, u32[]{:S(2)}) collective-permute-start(f32[7680]{0:T(1024)S(1)} %select_add_fusion.4), channel_id=1, source_target_pairs={{0,16},{1,17},{2,18},{3,19},{4,20},{5,21},{6,22},{7,23},{8,24},{9,... | collective-permute-start | bytes 92168 | tf_op jit(solution)/shard_map/ppermute | solution.py:18
  104.3 7.8 %collective-permute-start.6 = (f32[15360]{0:T(1024)S(1)}, f32[15360]{0:T(1024)S(1)}, u32[]{:S(2)}, u32[]{:S(2)}) collective-permute-start(f32[15360]{0:T(1024)S(1)} %maximum_select_fusion.4), channel_id=1, source_target_pairs={{0,8},{1,9},{2,10},{3,11},{4,12},{5,13},{6,14},{7,15},{8,0},{9,1},... | collective-permute-start | bytes 184328 | tf_op jit(solution)/shard_map/ppermute | solution.py:18
  112.1 8.8 %collective-permute-start.7 = (f32[30720]{0:T(1024)S(1)}, f32[30720]{0:T(1024)S(1)}, u32[]{:S(2)}, u32[]{:S(2)}) collective-permute-start(f32[30720]{0:T(1024)S(1)} %maximum_select_fusion.3), channel_id=1, source_target_pairs={{0,2},{1,3},{2,0},{3,1},{4,6},{5,7},{6,4},{7,5},{8,10},{9,11},{10,... | collective-permute-start | bytes 368648 | tf_op jit(solution)/shard_map/ppermute | solution.py:18
  120.9 10.1 %collective-permute-start.8 = (f32[61440]{0:T(1024)S(1)}, f32[61440]{0:T(1024)S(1)}, u32[]{:S(2)}, u32[]{:S(2)}) collective-permute-start(f32[61440]{0:T(1024)S(1)} %maximum_select_fusion.2), channel_id=1, source_target_pairs={{0,4},{1,5},{2,6},{3,7},{4,0},{5,1},{6,2},{7,3},{8,12},{9,13},{10,... | collective-permute-start | bytes 737288 | tf_op jit(solution)/shard_map/ppermute | solution.py:18
  131.0 20.9 %collective-permute-start.9 = (f32[122880]{0:T(1024)S(1)}, f32[122880]{0:T(1024)S(1)}, u32[]{:S(2)}, u32[]{:S(2)}) collective-permute-start(f32[122880]{0:T(1024)S(1)} %maximum_select_fusion.1), channel_id=1, source_target_pairs={{0,1},{1,0},{2,3},{3,2},{4,5},{5,4},{6,7},{7,6},{8,9},{9,8},{10,11... | collective-permute-start | bytes 1474568 | tf_op jit(solution)/shard_map/ppermute | solution.py:18
  165.5 4.4 copy-start.4
  191.8 238.5 %collective-permute-start.10 = (bf16[1024,256]{1,0:T(8,128)(2,1)}, bf16[1024,256]{1,0:T(8,128)(2,1)}, u32[]{:S(2)}, u32[]{:S(2)}) collective-permute-start(bf16[1024,256]{1,0:T(8,128)(2,1)} %fusion.14), channel_id=1, source_target_pairs={{0,64},{64,128},{128,192},{192,0},{1,65},{65,129},{129,193},{193,1... | collective-permute-start | bytes 1572872 | tf_op jit(solution)/shard_map/ppermute | solution.py:12
  423.6 9.2 %collective-permute-start.11 = (bf16[1024,256]{1,0:T(8,128)(2,1)S(1)}, bf16[1024,256]{1,0:T(8,128)(2,1)S(1)}, u32[]{:S(2)}, u32[]{:S(2)}) collective-permute-start(bf16[1024,256]{1,0:T(8,128)(2,1)S(1)} %add_convert_fusion), channel_id=1, source_target_pairs={{0,192},{64,0},{128,64},{192,128},{1,193},{65,1},{129,65},{193,129... | collective-permute-start | bytes 1572872 | tf_op jit(solution)/shard_map/ppermute | solution.py:12
Sparse Core Ops, SparseCore 0:
  10.4 161.5 all-gather.2
  176.1 245.8 reduce-scatter.1
